TPU v7x, 256 devices: a whole 4x4x8 slice. The times are simulated.
256 devices in a mesh: ctx: 32 (over y, z), tp: 8 (over x, core).
Axes of the slice: x: 4, y: 4, z: 8, core: 2. Of those that a mesh axis runs over, the one named last changes fastest.
Arguments:
- tokens: bfloat16 [16384, 4096], P('ctx', 'tp'), may hold values from -6 to 6
- qkv_blocks: bfloat16 [3, 4, 1024, 1024], P(None, None, None, 'tp'), may hold values from -0.046875 to 0.046875
- out_blocks: bfloat16 [4, 1024, 1024], P(None, 'tp'), may hold values from -0.046875 to 0.046875
- mix_factors: float32 [4, 4, 4, 4], replicated, may hold values from -4 to 4
- head_gain: float32 [4, 1024], P(None, 'tp'), may hold values from 0.1 to 1.9
Outputs:
- layer_out: bfloat16 [16384, 4096], P('ctx', 'tp')
All inputs are finite; a program needn't handle non-finite values.
Results may differ from a plain program's by a relative error of at most 0.025.
Values may be sent and summed in bfloat16 or wider, within the bound.
No kernel may reach another device: no remote copies, remote signals or barrier semaphores. Data moves between devices by JAX's collectives and lax.ppermute only.
A program may use at most 128 MiB of HBM per device.

v0:
```python
import functools
import jax
import jax.numpy as jnp
from jax import lax
from jax.sharding import PartitionSpec as P

PHM = 4
SPAN = 128
HEAD = 128
BLOCK = 1024
epsilon = 1e-06


def ring_gather(value, axis, devices, size, stride, before):
    here = lax.axis_index(axis)
    k_here = here // stride % size
    total = value.astype(jnp.float32)
    earlier = jnp.zeros_like(total)
    for shift in range(1, size):
        pairs = []
        for i in range(devices):
            k = i // stride % size
            pairs.append((i, i + ((k + shift) % size - k) * stride))
        got = lax.ppermute(value, axis, pairs).astype(jnp.float32)
        source = (k_here - shift) % size
        total = total + got
        earlier = earlier + jnp.where(source < before, got, 0.0)
    return (total, earlier)


def exclusive_prefix(value, axis, devices, row):
    here = lax.axis_index(axis)
    pos, col = (here % row, here // row)
    row_total, before = ring_gather(value.astype(jnp.bfloat16), axis, devices, row, 1, pos)
    _, rows_before = ring_gather(row_total, axis, devices, devices // row, row, col)
    return before + rows_before


def fold_weights(blocks, mixing):
    terms, rows, cols = blocks.shape
    folded = None
    for term_index in range(terms):
        part = (
            mixing[term_index][:, None, :, None]
            * blocks[term_index].astype(jnp.float32)[None, :, None, :]
        )
        folded = part if folded is None else folded + part
    return folded.reshape(PHM * rows, PHM * cols)


def project(whole, blocks, mixing):
    projections, terms, rows, cols = blocks.shape
    tok_rows = whole.shape[0]
    weights = jnp.transpose(blocks, (2, 0, 1, 3)).reshape(rows, projections * terms * cols)
    products = [
        jnp.dot(whole[:, c * rows : (c + 1) * rows], weights, preferred_element_type=jnp.float32)
        for c in range(PHM)
    ]
    outs = []
    for p in range(projections):
        blocks_out = []
        for r in range(PHM):
            summed = None
            for term_index in range(terms):
                at = (p * terms + term_index) * cols
                for c in range(PHM):
                    part = products[c][:, at : at + cols] * mixing[p, term_index, c, r]
                    summed = part if summed is None else summed + part
            blocks_out.append(summed.astype(jnp.bfloat16))
        outs.append(jnp.concatenate(blocks_out, axis=1))
    return lax.optimization_barrier(outs)


def on_device(ctx_devices, ctx_row, tokens, qkv_blocks, out_blocks, mix_factors, head_gain):
    col_width = qkv_blocks.shape[-1]
    w_out = fold_weights(out_blocks, mix_factors[3]).astype(jnp.bfloat16)
    whole = lax.all_gather(tokens, "tp", axis=1, tiled=True)
    tok_rows = whole.shape[0]
    local_heads = PHM * col_width // HEAD
    nblk = tok_rows // SPAN
    width = PHM * col_width
    key, value = project(whole, qkv_blocks[1:], mix_factors[1:3])
    key_heads = key.reshape(nblk, SPAN, local_heads, HEAD)
    value_heads = value.reshape(nblk, SPAN, local_heads, HEAD)
    states = jnp.einsum(
        "nshd,nshe->nhde", key_heads, value_heads, preferred_element_type=jnp.float32
    )
    totals = jnp.sum(states, axis=0)
    earlier_sum = exclusive_prefix(totals, "ctx", ctx_devices, ctx_row)
    (query,) = project(whole, qkv_blocks[:1], mix_factors[:1])
    query_heads = query.reshape(nblk, SPAN, local_heads, HEAD)
    scores = jnp.einsum(
        "nshd,nthd->nhst", query_heads, key_heads, preferred_element_type=jnp.float32
    )
    causal = jnp.arange(SPAN)[:, None] >= jnp.arange(SPAN)[None, :]
    scores = jnp.where(causal[None, None], scores, 0.0).astype(jnp.bfloat16)
    within = jnp.einsum("nhst,nthe->nshe", scores, value_heads, preferred_element_type=jnp.float32)
    prefixes = [earlier_sum]
    for n in range(1, nblk):
        prefixes.append(prefixes[-1] + states[n - 1])
    prefix = jnp.stack(prefixes, axis=0)
    prefix_hi = prefix.astype(jnp.bfloat16)
    prefix_lo = (prefix - prefix_hi.astype(jnp.float32)).astype(jnp.bfloat16)
    carried_out = jnp.einsum(
        "nshd,nhde->nshe",
        jnp.concatenate([query_heads, query_heads], axis=-1),
        jnp.concatenate([prefix_hi, prefix_lo], axis=-2),
        preferred_element_type=jnp.float32,
    )
    combined = within + carried_out
    mean_sq = jnp.mean(combined * combined, axis=-1, keepdims=True)
    normed = combined * lax.rsqrt(mean_sq + epsilon) * head_gain
    attn = normed.astype(jnp.bfloat16).reshape(tok_rows, PHM * col_width)
    partial_value = jnp.dot(attn, w_out, preferred_element_type=jnp.float32)
    reduced = lax.psum_scatter(
        partial_value.astype(jnp.bfloat16), "tp", scatter_dimension=1, tiled=True
    )
    return reduced


def ctx_row_of(mesh):
    n = mesh.shape["ctx"]
    return 8 if n % 8 == 0 else n


def solution(mesh):
    placed = (P("ctx", "tp"), P(None, None, None, "tp"), P(None, "tp", None), P(), P(None, "tp"))
    return jax.shard_map(
        functools.partial(on_device, mesh.shape["ctx"], ctx_row_of(mesh)),
        mesh=mesh,
        in_specs=placed,
        out_specs=P("ctx", "tp"),
        check_vma=False,
    )
```

profile of v0, /device:TPU:8, one launch (start us, length us, event | category | flops | bytes accessed | tf_op | source)
XLA Modules:
  0.0 269.7 jit_solution(15784364006472150208)
XLA Ops:
  6.5 0.7 all-gather.2.cloned.1.call-update
  7.5 1.6 slice-done
  9.1 2.7 copy.22
  11.8 1.3 copy.23
  13.1 0.2 bitcast_convert_fusion.3
  13.3 4.8 %add_convert_fusion = bf16[4,128,4,1024]{3,2,1,0:T(4,128)(2,1)S(1)} fusion(f32[128,1024]{1,0:T(8,128)S(1)} %get-tuple-element.15, f32[4,4]{1,0:T(4,128)S(1)} %get-tuple-element.212, f32[128,1024]{1,0:T(8,128)S(1)} %get-tuple-element.16, f32[4,4]{1,0:T(4,128)S(1)} %get-tuple-element.211, f32[128,1024]{1,0:T(8,128)S(1)} %get-tuple-element.14, ...), kind=kLoop, calls=%fused_computation | loop fusion | flops 16777216 | bytes 6291712 | tf_op jit(solution)/shard_map/convert_element_type | solution.py:76
  18.1 4.3 %copy.25 = bf16[64,8,4,1024]{3,1,2,0:T(8,128)(2,1)} copy(bf16[64,8,4,1024]{3,2,1,0:T(4,128)(2,1)S(1)} %bitcast.275) | data formatting | bytes 8388608
  22.5 0.6 fusion.59
  23.1 0.6 fusion.57
  23.7 0.7 fusion.55
  24.4 0.7 fusion.56
  25.1 0.7 fusion.49
  25.9 0.7 fusion.53
  26.6 0.7 fusion.54
  27.3 0.7 fusion.50
  28.1 0.7 fusion.51
  28.8 0.7 fusion.52
  29.5 0.7 fusion.58
  30.2 16.5 %all-gather.2.cloned.1.call-done = bf16[512,4096]{1,0:T(8,128)(2,1)} async-done(((bf16[512,512]{1,0:T(8,128)(2,1)}), bf16[512,4096]{1,0:T(8,128)(2,1)}) %all-gather.2.cloned.1.call-update) | async-done | bytes 4194320 | tf_op jit(solution)/shard_map/all_gather | solution.py:77
  46.7 2.7 fusion.11
  49.3 1.3 fusion.15
  50.6 1.3 fusion.19
  51.9 1.3 fusion.23
  53.2 9.7 %add_convert_fusion.10 = bf16[512,128]{1,0:T(8,128)(2,1)S(1)} fusion(f32[512,1024]{1,0:T(8,128)S(1)} %fusion.11, f32[512,1024]{1,0:T(8,128)S(1)} %fusion.15, f32[512,1024]{1,0:T(8,128)S(1)} %fusion.19, f32[512,1024]{1,0:T(8,128)S(1)} %fusion.23, f32[]{:T(128)} %bitcast.50, f32[]{:T(128)} %bitcast.49, f32[]{:T(128)} %bitcast.48, f32[]{:T(128)} %bitcast.47, ...), kind=kLoop, calls=%fused_computation.85 | loop fusion | flops 2097152 | bytes 4325440 | tf_op jit(solution)/shard_map/convert_element_type | solution.py:69
  63.0 10.2 %add_convert_fusion.11 = bf16[512,128]{1,0:T(8,128)(2,1)S(1)} fusion(f32[512,1024]{1,0:T(8,128)S(1)} %fusion.11, f32[512,1024]{1,0:T(8,128)S(1)} %fusion.15, f32[512,1024]{1,0:T(8,128)S(1)} %fusion.19, f32[512,1024]{1,0:T(8,128)S(1)} %fusion.23, f32[]{:T(128)} %bitcast.34, f32[]{:T(128)} %bitcast.33, f32[]{:T(128)} %bitcast.32, f32[]{:T(128)} %bitcast.31, ...), kind=kLoop, calls=%fused_computation.86 | loop fusion | flops 2097152 | bytes 4325440 | tf_op jit(solution)/shard_map/convert_element_type | solution.py:69
  73.2 10.3 %add_convert_fusion.5 = bf16[512,128]{1,0:T(8,128)(2,1)S(1)} fusion(f32[512,1024]{1,0:T(8,128)S(1)} %fusion.11, f32[512,1024]{1,0:T(8,128)S(1)} %fusion.15, f32[512,1024]{1,0:T(8,128)S(1)} %fusion.19, f32[512,1024]{1,0:T(8,128)S(1)} %fusion.23, f32[]{:T(128)} %bitcast.130, f32[]{:T(128)} %bitcast.129, f32[]{:T(128)} %bitcast.128, f32[]{:T(128)} %bitcast.127, ...), kind=kLoop, calls=%fused_computation.80 | loop fusion | flops 2097152 | bytes 4325440 | tf_op jit(solution)/shard_map/convert_element_type | solution.py:69
  83.5 10.5 %add_convert_fusion.6 = bf16[512,128]{1,0:T(8,128)(2,1)S(1)} fusion(f32[512,1024]{1,0:T(8,128)S(1)} %fusion.11, f32[512,1024]{1,0:T(8,128)S(1)} %fusion.15, f32[512,1024]{1,0:T(8,128)S(1)} %fusion.19, f32[512,1024]{1,0:T(8,128)S(1)} %fusion.23, f32[]{:T(128)} %bitcast.114, f32[]{:T(128)} %bitcast.113, f32[]{:T(128)} %bitcast.112, f32[]{:T(128)} %bitcast.111, ...), kind=kLoop, calls=%fused_computation.81 | loop fusion | flops 2097152 | bytes 4325440 | tf_op jit(solution)/shard_map/convert_element_type | solution.py:69
  94.1 10.3 %add_convert_fusion.7 = bf16[512,128]{1,0:T(8,128)(2,1)S(1)} fusion(f32[512,1024]{1,0:T(8,128)S(1)} %fusion.11, f32[512,1024]{1,0:T(8,128)S(1)} %fusion.15, f32[512,1024]{1,0:T(8,128)S(1)} %fusion.19, f32[512,1024]{1,0:T(8,128)S(1)} %fusion.23, f32[]{:T(128)} %bitcast.98, f32[]{:T(128)} %bitcast.97, f32[]{:T(128)} %bitcast.96, f32[]{:T(128)} %bitcast.95, ...), kind=kLoop, calls=%fused_computation.82 | loop fusion | flops 2097152 | bytes 4325440 | tf_op jit(solution)/shard_map/convert_element_type | solution.py:69
  104.4 10.4 %add_convert_fusion.8 = bf16[512,128]{1,0:T(8,128)(2,1)S(1)} fusion(f32[512,1024]{1,0:T(8,128)S(1)} %fusion.11, f32[512,1024]{1,0:T(8,128)S(1)} %fusion.15, f32[512,1024]{1,0:T(8,128)S(1)} %fusion.19, f32[512,1024]{1,0:T(8,128)S(1)} %fusion.23, f32[]{:T(128)} %bitcast.82, f32[]{:T(128)} %bitcast.81, f32[]{:T(128)} %bitcast.80, f32[]{:T(128)} %bitcast.79, ...), kind=kLoop, calls=%fused_computation.83 | loop fusion | flops 2097152 | bytes 4325440 | tf_op jit(solution)/shard_map/convert_element_type | solution.py:69
  114.8 10.5 %add_convert_fusion.9 = bf16[512,128]{1,0:T(8,128)(2,1)S(1)} fusion(f32[512,1024]{1,0:T(8,128)S(1)} %fusion.11, f32[512,1024]{1,0:T(8,128)S(1)} %fusion.15, f32[512,1024]{1,0:T(8,128)S(1)} %fusion.19, f32[512,1024]{1,0:T(8,128)S(1)} %fusion.23, f32[]{:T(128)} %bitcast.66, f32[]{:T(128)} %bitcast.65, f32[]{:T(128)} %bitcast.64, f32[]{:T(128)} %bitcast.63, ...), kind=kLoop, calls=%fused_computation.84 | loop fusion | flops 2097152 | bytes 4325440 | tf_op jit(solution)/shard_map/convert_element_type | solution.py:69
  125.3 9.9 %add_convert_fusion.12 = bf16[512,128]{1,0:T(8,128)(2,1)S(1)} fusion(f32[512,1024]{1,0:T(8,128)S(1)} %fusion.11, f32[512,1024]{1,0:T(8,128)S(1)} %fusion.15, f32[512,1024]{1,0:T(8,128)S(1)} %fusion.19, f32[512,1024]{1,0:T(8,128)S(1)} %fusion.23, f32[]{:T(128)} %bitcast.18, f32[]{:T(128)} %bitcast.17, f32[]{:T(128)} %bitcast.16, f32[]{:T(128)} %bitcast.15, ...), kind=kLoop, calls=%fused_computation.87 | loop fusion | flops 2097152 | bytes 4325440 | tf_op jit(solution)/shard_map/convert_element_type | solution.py:69
  135.5 0.3 copy.15
  135.9 1.0 fusion.60
  136.9 1.6 collective-permute-start
  138.5 2.5 collective-permute-start.1
  141.0 2.9 %collective-permute-start.2 = (bf16[4,128,128]{2,1,0:T(8,128)(2,1)}, bf16[4,128,128]{2,1,0:T(8,128)(2,1)S(1)}, u32[]{:S(2)}, u32[]{:S(2)}) collective-permute-start(bf16[4,128,128]{2,1,0:T(8,128)(2,1)} %get-tuple-element.213), channel_id=1, source_target_pairs={{0,24},{8,32},{16,40},{24,48},{32,56},{40,0},{48,8},{56,16},{64,88... | collective-permute-start | bytes 393224 | tf_op jit(solution)/shard_map/ppermute | solution.py:24
  144.0 2.0 collective-permute-start.3
  145.9 3.1 %collective-permute-start.4 = (bf16[4,128,128]{2,1,0:T(8,128)(2,1)}, bf16[4,128,128]{2,1,0:T(8,128)(2,1)}, u32[]{:S(2)}, u32[]{:S(2)}) collective-permute-start(bf16[4,128,128]{2,1,0:T(8,128)(2,1)} %get-tuple-element.213), channel_id=1, source_target_pairs={{0,40},{8,48},{16,56},{24,0},{32,8},{40,16},{48,24},{56,32},{64,10... | collective-permute-start | bytes 393224 | tf_op jit(solution)/shard_map/ppermute | solution.py:24
  149.1 2.0 fusion.13
  151.1 0.7 fusion.17
  151.8 0.7 fusion.21
  152.6 0.7 fusion.9
  153.3 10.5 %add_convert_fusion.1 = bf16[512,128]{0,1:T(8,128)(2,1)S(1)} fusion(f32[512,512]{0,1:T(8,128)S(1)} %fusion.9, f32[512,512]{0,1:T(8,128)S(1)} %fusion.13, f32[512,512]{0,1:T(8,128)S(1)} %fusion.17, f32[512,512]{0,1:T(8,128)S(1)} %fusion.21, f32[]{:T(128)} %bitcast.197, f32[]{:T(128)} %bitcast.196, f32[]{:T(128)} %bitcast.195, f32[]{:T(128)} %bitcast.194, ...), kind=kLoop, calls=%fused_computation.76 | loop fusion | flops 2097152 | bytes 4325440 | tf_op jit(solution)/shard_map/convert_element_type | solution.py:69
  163.8 10.4 %add_convert_fusion.2 = bf16[512,128]{0,1:T(8,128)(2,1)S(1)} fusion(f32[512,512]{0,1:T(8,128)S(1)} %fusion.9, f32[512,512]{0,1:T(8,128)S(1)} %fusion.13, f32[512,512]{0,1:T(8,128)S(1)} %fusion.17, f32[512,512]{0,1:T(8,128)S(1)} %fusion.21, f32[]{:T(128)} %bitcast.181, f32[]{:T(128)} %bitcast.180, f32[]{:T(128)} %bitcast.179, f32[]{:T(128)} %bitcast.178, ...), kind=kLoop, calls=%fused_computation.77 | loop fusion | flops 2097152 | bytes 4325440 | tf_op jit(solution)/shard_map/convert_element_type | solution.py:69
  174.2 10.5 %add_convert_fusion.3 = bf16[512,128]{0,1:T(8,128)(2,1)S(1)} fusion(f32[512,512]{0,1:T(8,128)S(1)} %fusion.9, f32[512,512]{0,1:T(8,128)S(1)} %fusion.13, f32[512,512]{0,1:T(8,128)S(1)} %fusion.17, f32[512,512]{0,1:T(8,128)S(1)} %fusion.21, f32[]{:T(128)} %bitcast.165, f32[]{:T(128)} %bitcast.164, f32[]{:T(128)} %bitcast.163, f32[]{:T(128)} %bitcast.162, ...), kind=kLoop, calls=%fused_computation.78 | loop fusion | flops 2097152 | bytes 4325440 | tf_op jit(solution)/shard_map/convert_element_type | solution.py:69
  184.7 3.5 %collective-permute-start.5 = (bf16[4,128,128]{2,1,0:T(8,128)(2,1)}, bf16[4,128,128]{2,1,0:T(8,128)(2,1)}, u32[]{:S(2)}, u32[]{:S(2)}) collective-permute-start(bf16[4,128,128]{2,1,0:T(8,128)(2,1)} %get-tuple-element.213), channel_id=1, source_target_pairs={{0,48},{8,56},{16,0},{24,8},{32,16},{40,24},{48,32},{56,40},{64,11... | collective-permute-start | bytes 393224 | tf_op jit(solution)/shard_map/ppermute | solution.py:24
  188.2 1.4 collective-permute-start.6
  189.6 10.5 %add_convert_fusion.4 = bf16[512,128]{0,1:T(8,128)(2,1)S(1)} fusion(f32[512,512]{0,1:T(8,128)S(1)} %fusion.9, f32[512,512]{0,1:T(8,128)S(1)} %fusion.13, f32[512,512]{0,1:T(8,128)S(1)} %fusion.17, f32[512,512]{0,1:T(8,128)S(1)} %fusion.21, f32[]{:T(128)} %bitcast.149, f32[]{:T(128)} %bitcast.148, f32[]{:T(128)} %bitcast.147, f32[]{:T(128)} %bitcast.146, ...), kind=kLoop, calls=%fused_computation.79 | loop fusion | flops 2097152 | bytes 4325440 | tf_op jit(solution)/shard_map/convert_element_type | solution.py:69
  200.3 0.4 copy.18
  200.7 2.0 convert_add_fusion
  202.7 1.5 collective-permute-start.7
  204.2 1.1 collective-permute-start.8
  205.3 2.1 collective-permute-start.9
  207.5 1.6 fusion.2
  209.1 3.0 %collective-permute-done.7 = f32[4,128,128]{2,1,0:T(8,128)S(1)} collective-permute-done((f32[4,128,128]{2,1,0:T(8,128)}, f32[4,128,128]{2,1,0:T(8,128)S(1)}, u32[]{:S(2)}, u32[]{:S(2)}) %collective-permute-start.7) | collective-permute-done | bytes 262176 | tf_op jit(solution)/shard_map/ppermute | solution.py:24
  212.1 2.9 %collective-permute-done.8 = f32[4,128,128]{2,1,0:T(8,128)S(1)} collective-permute-done((f32[4,128,128]{2,1,0:T(8,128)}, f32[4,128,128]{2,1,0:T(8,128)S(1)}, u32[]{:S(2)}, u32[]{:S(2)}) %collective-permute-start.8) | collective-permute-done | bytes 262176 | tf_op jit(solution)/shard_map/ppermute | solution.py:24
  215.0 2.2 collective-permute-done.9
  217.2 1.3 fusion.44
  218.8 0.9 copy-done.3
  219.7 0.5 multiply_reduce_fusion
  220.4 0.2 multiply_convert_fusion
  220.6 0.3 copy.20
  220.9 6.6 %convolution_convert_fusion = bf16[512,4096]{1,0:T(8,128)(2,1)} fusion(bf16[512,4096]{1,0:T(8,128)(2,1)} %bitcast.276, bf16[64,8,4,128]{3,2,1,0:T(4,128)(2,1)S(1)} %bitcast.287), kind=kOutput, calls=%fused_computation.1 | convolution fusion | flops 2149580800 | bytes 8912896 | tf_op jit(solution)/shard_map/dot_general | solution.py:114
  227.5 35.3 %reduce-scatter.2.cloned.1.call-done = bf16[512,512]{1,0:T(8,128)(2,1)} async-done(((bf16[512,4096]{1,0:T(8,128)(2,1)}), bf16[512,512]{1,0:T(8,128)(2,1)}) %reduce-scatter.2.cloned.1.call-update) | async-done | bytes 524304 | tf_op jit(solution)/shard_map/reduce_scatter | solution.py:115
  (39 shorter events, 1.1 us)
Async XLA Ops:
  6.5 40.1 %all-gather.2.cloned.1.call-start = ((), (), s32[]{:S(2)}) async-start(), calls=%async_computation.1 | async-start | bytes 4718592 | tf_op jit(solution)/shard_map/all_gather | solution.py:77
  7.3 255.6 %reduce-scatter.2.cloned.1.call-start = ((), (), s32[]{:S(2)}) async-start(), calls=%async_computation.2 | async-start | bytes 4718592 | tf_op jit(solution)/shard_map/reduce_scatter | solution.py:115
  7.5 1.6 slice-start
  9.1 2.7 slice-start.1
  11.8 1.3 copy-start.4
  11.8 1.3 copy-start.1
  18.1 28.5 %copy-start = (bf16[2,4,1024,128]{2,3,1,0:T(8,128)(2,1)S(1)}, bf16[2,4,1024,128]{2,3,1,0:T(8,128)(2,1)}, u32[]{:S(2)}) copy-start(bf16[2,4,1024,128]{2,3,1,0:T(8,128)(2,1)} %copy.22) | copy-start | bytes 6291460
  46.7 2.7 copy-start.6
  135.5 13.6 %copy-start.2 = (bf16[1,4,1024,128]{2,3,1,0:T(8,128)(2,1)S(1)}, bf16[1,4,1024,128]{2,3,1,0:T(8,128)(2,1)}, u32[]{:S(2)}) copy-start(bf16[1,4,1024,128]{2,3,1,0:T(8,128)(2,1)} %copy.23) | copy-start | bytes 3145732
  135.9 15.1 %copy-start.7 = (bf16[512,4096]{1,0:T(8,128)(2,1)S(1)}, bf16[512,4096]{1,0:T(8,128)(2,1)}, u32[]{:S(2)}) copy-start(bf16[512,4096]{1,0:T(8,128)(2,1)} %all-gather.2.cloned.1.call-done) | copy-start | bytes 12582916
  136.9 47.8 %collective-permute-start = (bf16[4,128,128]{2,1,0:T(8,128)(2,1)}, bf16[4,128,128]{2,1,0:T(8,128)(2,1)S(1)}, u32[]{:S(2)}, u32[]{:S(2)}) collective-permute-start(bf16[4,128,128]{2,1,0:T(8,128)(2,1)} %get-tuple-element.213), channel_id=1, source_target_pairs={{0,8},{8,16},{16,24},{24,32},{32,40},{40,48},{48,56},{56,0},{64,72... | collective-permute-start | bytes 393224 | tf_op jit(solution)/shard_map/ppermute | solution.py:24
  138.5 49.7 %collective-permute-start.1 = (bf16[4,128,128]{2,1,0:T(8,128)(2,1)}, bf16[4,128,128]{2,1,0:T(8,128)(2,1)S(1)}, u32[]{:S(2)}, u32[]{:S(2)}) collective-permute-start(bf16[4,128,128]{2,1,0:T(8,128)(2,1)} %get-tuple-element.213), channel_id=1, source_target_pairs={{0,16},{8,24},{16,32},{24,40},{32,48},{40,56},{48,0},{56,8},{64,80... | collective-permute-start | bytes 393224 | tf_op jit(solution)/shard_map/ppermute | solution.py:24
  141.0 59.7 %collective-permute-start.2 = (bf16[4,128,128]{2,1,0:T(8,128)(2,1)}, bf16[4,128,128]{2,1,0:T(8,128)(2,1)S(1)}, u32[]{:S(2)}, u32[]{:S(2)}) collective-permute-start(bf16[4,128,128]{2,1,0:T(8,128)(2,1)} %get-tuple-element.213), channel_id=1, source_target_pairs={{0,24},{8,32},{16,40},{24,48},{32,56},{40,0},{48,8},{56,16},{64,88... | collective-permute-start | bytes 393224 | tf_op jit(solution)/shard_map/ppermute | solution.py:24
  144.0 56.7 %collective-permute-start.3 = (bf16[4,128,128]{2,1,0:T(8,128)(2,1)}, bf16[4,128,128]{2,1,0:T(8,128)(2,1)}, u32[]{:S(2)}, u32[]{:S(2)}) collective-permute-start(bf16[4,128,128]{2,1,0:T(8,128)(2,1)} %get-tuple-element.213), channel_id=1, source_target_pairs={{0,32},{8,40},{16,48},{24,56},{32,0},{40,8},{48,16},{56,24},{64,96... | collective-permute-start | bytes 393224 | tf_op jit(solution)/shard_map/ppermute | solution.py:24
  145.9 54.7 %collective-permute-start.4 = (bf16[4,128,128]{2,1,0:T(8,128)(2,1)}, bf16[4,128,128]{2,1,0:T(8,128)(2,1)}, u32[]{:S(2)}, u32[]{:S(2)}) collective-permute-start(bf16[4,128,128]{2,1,0:T(8,128)(2,1)} %get-tuple-element.213), channel_id=1, source_target_pairs={{0,40},{8,48},{16,56},{24,0},{32,8},{40,16},{48,24},{56,32},{64,10... | collective-permute-start | bytes 393224 | tf_op jit(solution)/shard_map/ppermute | solution.py:24
  184.7 16.0 %collective-permute-start.5 = (bf16[4,128,128]{2,1,0:T(8,128)(2,1)}, bf16[4,128,128]{2,1,0:T(8,128)(2,1)}, u32[]{:S(2)}, u32[]{:S(2)}) collective-permute-start(bf16[4,128,128]{2,1,0:T(8,128)(2,1)} %get-tuple-element.213), channel_id=1, source_target_pairs={{0,48},{8,56},{16,0},{24,8},{32,16},{40,24},{48,32},{56,40},{64,11... | collective-permute-start | bytes 393224 | tf_op jit(solution)/shard_map/ppermute | solution.py:24
  188.2 12.5 %collective-permute-start.6 = (bf16[4,128,128]{2,1,0:T(8,128)(2,1)}, bf16[4,128,128]{2,1,0:T(8,128)(2,1)}, u32[]{:S(2)}, u32[]{:S(2)}) collective-permute-start(bf16[4,128,128]{2,1,0:T(8,128)(2,1)} %get-tuple-element.213), channel_id=1, source_target_pairs={{0,56},{8,0},{16,8},{24,16},{32,24},{40,32},{48,40},{56,48},{64,12... | collective-permute-start | bytes 393224 | tf_op jit(solution)/shard_map/ppermute | solution.py:24
  202.7 9.4 %collective-permute-start.7 = (f32[4,128,128]{2,1,0:T(8,128)}, f32[4,128,128]{2,1,0:T(8,128)S(1)}, u32[]{:S(2)}, u32[]{:S(2)}) collective-permute-start(f32[4,128,128]{2,1,0:T(8,128)} %convert_add_fusion), channel_id=1, source_target_pairs={{0,64},{8,72},{16,80},{24,88},{32,96},{40,104},{48,112},{56,120},{... | collective-permute-start | bytes 786440 | tf_op jit(solution)/shard_map/ppermute | solution.py:24
  204.2 10.8 %collective-permute-start.8 = (f32[4,128,128]{2,1,0:T(8,128)}, f32[4,128,128]{2,1,0:T(8,128)S(1)}, u32[]{:S(2)}, u32[]{:S(2)}) collective-permute-start(f32[4,128,128]{2,1,0:T(8,128)} %convert_add_fusion), channel_id=1, source_target_pairs={{0,128},{8,136},{16,144},{24,152},{32,160},{40,168},{48,176},{56,1... | collective-permute-start | bytes 786440 | tf_op jit(solution)/shard_map/ppermute | solution.py:24
  205.3 11.9 %collective-permute-start.9 = (f32[4,128,128]{2,1,0:T(8,128)}, f32[4,128,128]{2,1,0:T(8,128)}, u32[]{:S(2)}, u32[]{:S(2)}) collective-permute-start(f32[4,128,128]{2,1,0:T(8,128)} %convert_add_fusion), channel_id=1, source_target_pairs={{0,192},{8,200},{16,208},{24,216},{32,224},{40,232},{48,240},{56,2... | collective-permute-start | bytes 786440 | tf_op jit(solution)/shard_map/ppermute | solution.py:24
  218.5 1.2 copy-start.3
  219.7 0.7 copy-start.5
Sparse Core Ops, SparseCore 0:
  9.2 37.4 all-gather.1
  227.6 35.1 reduce-scatter.1
where the time goes:
time: 272 us; the launch traced here: 270 us
  other arithmetic  133 us (49%)
  waiting for transfers between devices  60.6 us (22%)
  starting transfers between devices  21.8 us (8%)
  matrix products  20.4 us (7%)
  local copies, waits for them, and re-layouts  20 us (7%)
  between operations  14 us (5%)
    convert_element_type x12, other arithmetic, project(): blocks_out.append(summed.astype(jnp.bfloat16))  124 us
    reduce_scatter x1, waiting for transfers between devices, on_device(): lax.psum_scatter(partial_value.astype(jnp.bfloat16), 'tp', scatter_dimens...  35.3 us
    ppermute x10, starting transfers between devices, ring_gather(): got = lax.ppermute(value, axis, pairs).astype(jnp.float32)  21.8 us
    all_gather x1, waiting for transfers between devices, on_device(): whole = lax.all_gather(tokens, 'tp', axis=1, tiled=True)  16.5 us
    dot_general x8, matrix products, project(): jnp.dot(whole[:, c * rows:(c + 1) * rows], weights, preferred_element_typ...  10.7 us
    unnamed x19, local copies, waits for them, and re-layouts  9.4 us
    ppermute x10, waiting for transfers between devices, ring_gather(): got = lax.ppermute(value, axis, pairs).astype(jnp.float32)  8.1 us
    slice x11, local copies, waits for them, and re-layouts, project(): part = products[c][:, at:at + cols] * mixing[p, term_index, c, r]  7.7 us
  transfers between devices with their start and end apart: 12, of which 5 were waited for; matrix products, arithmetic and copies ran while one was open for 26% of the time, Pallas kernels for 0%

commit v1 on v0

--- a/solution.py
+++ b/solution.py
@@ -74,7 +74,9 @@
 def on_device(ctx_devices, ctx_row, tokens, qkv_blocks, out_blocks, mix_factors, head_gain):
     col_width = qkv_blocks.shape[-1]
     w_out = fold_weights(out_blocks, mix_factors[3]).astype(jnp.bfloat16)
-    whole = lax.all_gather(tokens, "tp", axis=1, tiled=True)
+    length = lax.axis_size("tp")
+    repeats = [length if d == 1 else 1 for d in range(tokens.ndim)]
+    whole = lax.all_to_all(jnp.tile(tokens, repeats), "tp", split_axis=1, concat_axis=1, tiled=True)
     tok_rows = whole.shape[0]
     local_heads = PHM * col_width // HEAD
     nblk = tok_rows // SPAN

time: 272 us -> 297 us (1.092)
  local copies, waits for them, and re-layouts: 20 us -> 30.1 us
  waiting for transfers between devices: 60.6 us -> 69.9 us
  starting transfers between devices: 21.8 us -> 28 us
    all_to_all x0 -> x1, waiting for transfers between devices: none -> 26.8 us  [on_device(): lax.all_to_all(jnp.tile(tokens, repeats), 'tp', split_axis=1, concat_axis...]
    all_gather x1 -> x0, waiting for transfers between devices: 16.5 us -> none  [on_device(): whole = lax.all_gather(tokens, 'tp', axis=1, tiled=True)]
    all_to_all x0 -> x1, local copies, waits for them, and re-layouts: none -> 6.51 us  [on_device(): lax.all_to_all(jnp.tile(tokens, repeats), 'tp', split_axis=1, concat_axis...]
    all_to_all x0 -> x1, starting transfers between devices: none -> 4.57 us  [on_device(): lax.all_to_all(jnp.tile(tokens, repeats), 'tp', split_axis=1, concat_axis...]
    another operation x0 -> x1, local copies, waits for them, and re-layouts: none -> 3.4 us  [on_device(): jnp.tile(tokens, repeats)]
  transfers between devices with their start and end apart: 12 -> 12, of which waited for: 5 -> 5; matrix products, arithmetic and copies ran while one was open for 26% -> 23% of each run, Pallas kernels for 0% -> 0%
where the time goes in v1:
time: 297 us; the launch traced here: 295 us
  other arithmetic  133 us (45%)
  waiting for transfers between devices  69.9 us (24%)
  local copies, waits for them, and re-layouts  30.1 us (10%)
  starting transfers between devices  28 us (9%)
  matrix products  20.3 us (7%)
  between operations  14 us (5%)
    convert_element_type x12, other arithmetic, project(): blocks_out.append(summed.astype(jnp.bfloat16))  124 us
    reduce_scatter x1, waiting for transfers between devices, on_device(): lax.psum_scatter(partial_value.astype(jnp.bfloat16), 'tp', scatter_dimens...  35.9 us
    all_to_all x1, waiting for transfers between devices, on_device(): lax.all_to_all(jnp.tile(tokens, repeats), 'tp', split_axis=1, concat_axis...  26.8 us
    ppermute x10, starting transfers between devices, ring_gather(): got = lax.ppermute(value, axis, pairs).astype(jnp.float32)  23.4 us
    dot_general x8, matrix products, project(): jnp.dot(whole[:, c * rows:(c + 1) * rows], weights, preferred_element_typ...  10.6 us
    unnamed x19, local copies, waits for them, and re-layouts  9.45 us
    slice x11, local copies, waits for them, and re-layouts, project(): part = products[c][:, at:at + cols] * mixing[p, term_index, c, r]  7.75 us
    ppermute x10, waiting for transfers between devices, ring_gather(): got = lax.ppermute(value, axis, pairs).astype(jnp.float32)  7.19 us
  transfers between devices with their start and end apart: 12, of which 5 were waited for; matrix products, arithmetic and copies ran while one was open for 23% of the time, Pallas kernels for 0%

profile of v1, /device:TPU:8, one launch (start us, length us, event | category | flops | bytes accessed | tf_op | source)
XLA Modules:
  0.0 295.2 jit_solution(10481345619869007094)
XLA Ops:
  6.5 3.4 %tile.2 = bf16[512,8,512]{2,0,1:T(8,128)(2,1)} broadcast(bf16[512,512]{1,0:T(8,128)(2,1)} %param.5), dimensions={0,2} | broadcast | bytes 4718592 | tf_op jit(solution)/shard_map/tile | solution.py:79
  9.9 4.6 %all-to-all-start = ((bf16[512,8,512]{2,0,1:T(8,128)(2,1)}), bf16[512,8,512]{2,0,1:T(8,128)(2,1)}, u32[]{:S(2)}, u32[]{:S(2)}) async-start(bf16[512,8,512]{2,0,1:T(8,128)(2,1)} %tile.2), calls=%async_computation | async-start | bytes 8388608 | tf_op jit(solution)/shard_map/all_to_all | solution.py:79
  14.8 1.6 slice-done
  16.3 2.8 copy.45
  19.1 1.3 copy.46
  20.7 4.6 %add_convert_fusion = bf16[4,128,4,1024]{3,2,1,0:T(4,128)(2,1)S(1)} fusion(f32[128,1024]{1,0:T(8,128)S(1)} %get-tuple-element.15, f32[4,4]{1,0:T(4,128)S(1)} %get-tuple-element.212, f32[128,1024]{1,0:T(8,128)S(1)} %get-tuple-element.16, f32[4,4]{1,0:T(4,128)S(1)} %get-tuple-element.211, f32[128,1024]{1,0:T(8,128)S(1)} %get-tuple-element.14, ...), kind=kLoop, calls=%fused_computation | loop fusion | flops 16777216 | bytes 6291712 | tf_op jit(solution)/shard_map/convert_element_type | solution.py:76
  25.3 4.2 %copy.48 = bf16[64,8,4,1024]{3,1,2,0:T(8,128)(2,1)} copy(bf16[64,8,4,1024]{3,2,1,0:T(4,128)(2,1)S(1)} %bitcast.276) | data formatting | bytes 8388608
  29.6 0.6 fusion.59
  30.2 0.6 fusion.57
  30.8 0.7 fusion.49
  31.6 0.7 fusion.50
  32.3 0.7 fusion.51
  33.0 0.7 fusion.52
  33.7 0.7 fusion.53
  34.5 0.7 fusion.54
  35.2 0.7 fusion.56
  35.9 0.7 fusion.55
  36.6 0.7 fusion.58
  37.4 26.8 %all-to-all-done = bf16[512,8,512]{2,0,1:T(8,128)(2,1)} async-done(((bf16[512,8,512]{2,0,1:T(8,128)(2,1)}), bf16[512,8,512]{2,0,1:T(8,128)(2,1)}, u32[]{:S(2)}, u32[]{:S(2)}) %all-to-all-start) | async-done | bytes 4194336 | tf_op jit(solution)/shard_map/all_to_all | solution.py:79
  64.2 6.5 %copy.32 = bf16[512,8,512]{0,2,1:T(8,128)(2,1)} copy(bf16[512,8,512]{2,0,1:T(8,128)(2,1)} %all-to-all-done) | data formatting | bytes 8388608 | tf_op jit(solution)/shard_map/all_to_all | solution.py:79
  70.7 2.7 fusion.11
  73.4 1.3 fusion.15
  74.7 1.3 fusion.19
  76.0 1.3 fusion.23
  77.3 10.2 %add_convert_fusion.8 = bf16[512,128]{1,0:T(8,128)(2,1)S(1)} fusion(f32[512,1024]{1,0:T(8,128)S(1)} %fusion.11, f32[512,1024]{1,0:T(8,128)S(1)} %fusion.15, f32[512,1024]{1,0:T(8,128)S(1)} %fusion.19, f32[512,1024]{1,0:T(8,128)S(1)} %fusion.23, f32[]{:T(128)} %bitcast.83, f32[]{:T(128)} %bitcast.82, f32[]{:T(128)} %bitcast.81, f32[]{:T(128)} %bitcast.80, ...), kind=kLoop, calls=%fused_computation.83 | loop fusion | flops 2097152 | bytes 4325440 | tf_op jit(solution)/shard_map/convert_element_type | solution.py:69
  87.5 10.2 %add_convert_fusion.7 = bf16[512,128]{1,0:T(8,128)(2,1)S(1)} fusion(f32[512,1024]{1,0:T(8,128)S(1)} %fusion.11, f32[512,1024]{1,0:T(8,128)S(1)} %fusion.15, f32[512,1024]{1,0:T(8,128)S(1)} %fusion.19, f32[512,1024]{1,0:T(8,128)S(1)} %fusion.23, f32[]{:T(128)} %bitcast.99, f32[]{:T(128)} %bitcast.98, f32[]{:T(128)} %bitcast.97, f32[]{:T(128)} %bitcast.96, ...), kind=kLoop, calls=%fused_computation.82 | loop fusion | flops 2097152 | bytes 4325440 | tf_op jit(solution)/shard_map/convert_element_type | solution.py:69
  97.7 10.2 %add_convert_fusion.6 = bf16[512,128]{1,0:T(8,128)(2,1)S(1)} fusion(f32[512,1024]{1,0:T(8,128)S(1)} %fusion.11, f32[512,1024]{1,0:T(8,128)S(1)} %fusion.15, f32[512,1024]{1,0:T(8,128)S(1)} %fusion.19, f32[512,1024]{1,0:T(8,128)S(1)} %fusion.23, f32[]{:T(128)} %bitcast.115, f32[]{:T(128)} %bitcast.114, f32[]{:T(128)} %bitcast.113, f32[]{:T(128)} %bitcast.112, ...), kind=kLoop, calls=%fused_computation.81 | loop fusion | flops 2097152 | bytes 4325440 | tf_op jit(solution)/shard_map/convert_element_type | solution.py:69
  107.9 10.4 %add_convert_fusion.5 = bf16[512,128]{1,0:T(8,128)(2,1)S(1)} fusion(f32[512,1024]{1,0:T(8,128)S(1)} %fusion.11, f32[512,1024]{1,0:T(8,128)S(1)} %fusion.15, f32[512,1024]{1,0:T(8,128)S(1)} %fusion.19, f32[512,1024]{1,0:T(8,128)S(1)} %fusion.23, f32[]{:T(128)} %bitcast.131, f32[]{:T(128)} %bitcast.130, f32[]{:T(128)} %bitcast.129, f32[]{:T(128)} %bitcast.128, ...), kind=kLoop, calls=%fused_computation.80 | loop fusion | flops 2097152 | bytes 4325440 | tf_op jit(solution)/shard_map/convert_element_type | solution.py:69
  118.3 10.3 %add_convert_fusion.11 = bf16[512,128]{1,0:T(8,128)(2,1)S(1)} fusion(f32[512,1024]{1,0:T(8,128)S(1)} %fusion.11, f32[512,1024]{1,0:T(8,128)S(1)} %fusion.15, f32[512,1024]{1,0:T(8,128)S(1)} %fusion.19, f32[512,1024]{1,0:T(8,128)S(1)} %fusion.23, f32[]{:T(128)} %bitcast.35, f32[]{:T(128)} %bitcast.34, f32[]{:T(128)} %bitcast.33, f32[]{:T(128)} %bitcast.32, ...), kind=kLoop, calls=%fused_computation.86 | loop fusion | flops 2097152 | bytes 4325440 | tf_op jit(solution)/shard_map/convert_element_type | solution.py:69
  128.6 10.3 %add_convert_fusion.10 = bf16[512,128]{1,0:T(8,128)(2,1)S(1)} fusion(f32[512,1024]{1,0:T(8,128)S(1)} %fusion.11, f32[512,1024]{1,0:T(8,128)S(1)} %fusion.15, f32[512,1024]{1,0:T(8,128)S(1)} %fusion.19, f32[512,1024]{1,0:T(8,128)S(1)} %fusion.23, f32[]{:T(128)} %bitcast.51, f32[]{:T(128)} %bitcast.50, f32[]{:T(128)} %bitcast.49, f32[]{:T(128)} %bitcast.48, ...), kind=kLoop, calls=%fused_computation.85 | loop fusion | flops 2097152 | bytes 4325440 | tf_op jit(solution)/shard_map/convert_element_type | solution.py:69
  138.9 10.3 %add_convert_fusion.9 = bf16[512,128]{1,0:T(8,128)(2,1)S(1)} fusion(f32[512,1024]{1,0:T(8,128)S(1)} %fusion.11, f32[512,1024]{1,0:T(8,128)S(1)} %fusion.15, f32[512,1024]{1,0:T(8,128)S(1)} %fusion.19, f32[512,1024]{1,0:T(8,128)S(1)} %fusion.23, f32[]{:T(128)} %bitcast.67, f32[]{:T(128)} %bitcast.66, f32[]{:T(128)} %bitcast.65, f32[]{:T(128)} %bitcast.64, ...), kind=kLoop, calls=%fused_computation.84 | loop fusion | flops 2097152 | bytes 4325440 | tf_op jit(solution)/shard_map/convert_element_type | solution.py:69
  149.2 10.5 %add_convert_fusion.12 = bf16[512,128]{1,0:T(8,128)(2,1)S(1)} fusion(f32[512,1024]{1,0:T(8,128)S(1)} %fusion.11, f32[512,1024]{1,0:T(8,128)S(1)} %fusion.15, f32[512,1024]{1,0:T(8,128)S(1)} %fusion.19, f32[512,1024]{1,0:T(8,128)S(1)} %fusion.23, f32[]{:T(128)} %bitcast.19, f32[]{:T(128)} %bitcast.18, f32[]{:T(128)} %bitcast.17, f32[]{:T(128)} %bitcast.16, ...), kind=kLoop, calls=%fused_computation.87 | loop fusion | flops 2097152 | bytes 4325440 | tf_op jit(solution)/shard_map/convert_element_type | solution.py:69
  160.0 0.3 copy.38
  160.4 1.0 fusion.60
  161.4 1.9 collective-permute-start
  163.3 3.3 %collective-permute-start.1 = (bf16[4,128,128]{2,1,0:T(8,128)(2,1)}, bf16[4,128,128]{2,1,0:T(8,128)(2,1)S(1)}, u32[]{:S(2)}, u32[]{:S(2)}) collective-permute-start(bf16[4,128,128]{2,1,0:T(8,128)(2,1)} %get-tuple-element.213), channel_id=1, source_target_pairs={{0,16},{8,24},{16,32},{24,40},{32,48},{40,56},{48,0},{56,8},{64,80... | collective-permute-start | bytes 393224 | tf_op jit(solution)/shard_map/ppermute | solution.py:24
  166.6 4.0 %collective-permute-start.2 = (bf16[4,128,128]{2,1,0:T(8,128)(2,1)}, bf16[4,128,128]{2,1,0:T(8,128)(2,1)S(1)}, u32[]{:S(2)}, u32[]{:S(2)}) collective-permute-start(bf16[4,128,128]{2,1,0:T(8,128)(2,1)} %get-tuple-element.213), channel_id=1, source_target_pairs={{0,24},{8,32},{16,40},{24,48},{32,56},{40,0},{48,8},{56,16},{64,88... | collective-permute-start | bytes 393224 | tf_op jit(solution)/shard_map/ppermute | solution.py:24
  170.6 0.5 collective-permute-start.3
  171.1 4.9 %collective-permute-start.4 = (bf16[4,128,128]{2,1,0:T(8,128)(2,1)}, bf16[4,128,128]{2,1,0:T(8,128)(2,1)}, u32[]{:S(2)}, u32[]{:S(2)}) collective-permute-start(bf16[4,128,128]{2,1,0:T(8,128)(2,1)} %get-tuple-element.213), channel_id=1, source_target_pairs={{0,40},{8,48},{16,56},{24,0},{32,8},{40,16},{48,24},{56,32},{64,10... | collective-permute-start | bytes 393224 | tf_op jit(solution)/shard_map/ppermute | solution.py:24
  176.1 1.9 fusion.13
  178.0 0.7 fusion.17
  178.7 0.7 fusion.21
  179.5 0.7 fusion.9
  180.2 10.3 %add_convert_fusion.3 = bf16[512,128]{0,1:T(8,128)(2,1)S(1)} fusion(f32[512,512]{0,1:T(8,128)S(1)} %fusion.9, f32[512,512]{0,1:T(8,128)S(1)} %fusion.13, f32[512,512]{0,1:T(8,128)S(1)} %fusion.17, f32[512,512]{0,1:T(8,128)S(1)} %fusion.21, f32[]{:T(128)} %bitcast.166, f32[]{:T(128)} %bitcast.165, f32[]{:T(128)} %bitcast.164, f32[]{:T(128)} %bitcast.163, ...), kind=kLoop, calls=%fused_computation.78 | loop fusion | flops 2097152 | bytes 4325440 | tf_op jit(solution)/shard_map/convert_element_type | solution.py:69
  190.5 10.4 %add_convert_fusion.2 = bf16[512,128]{0,1:T(8,128)(2,1)S(1)} fusion(f32[512,512]{0,1:T(8,128)S(1)} %fusion.9, f32[512,512]{0,1:T(8,128)S(1)} %fusion.13, f32[512,512]{0,1:T(8,128)S(1)} %fusion.17, f32[512,512]{0,1:T(8,128)S(1)} %fusion.21, f32[]{:T(128)} %bitcast.182, f32[]{:T(128)} %bitcast.181, f32[]{:T(128)} %bitcast.180, f32[]{:T(128)} %bitcast.179, ...), kind=kLoop, calls=%fused_computation.77 | loop fusion | flops 2097152 | bytes 4325440 | tf_op jit(solution)/shard_map/convert_element_type | solution.py:69
  200.9 10.5 %add_convert_fusion.1 = bf16[512,128]{0,1:T(8,128)(2,1)S(1)} fusion(f32[512,512]{0,1:T(8,128)S(1)} %fusion.9, f32[512,512]{0,1:T(8,128)S(1)} %fusion.13, f32[512,512]{0,1:T(8,128)S(1)} %fusion.17, f32[512,512]{0,1:T(8,128)S(1)} %fusion.21, f32[]{:T(128)} %bitcast.198, f32[]{:T(128)} %bitcast.197, f32[]{:T(128)} %bitcast.196, f32[]{:T(128)} %bitcast.195, ...), kind=kLoop, calls=%fused_computation.76 | loop fusion | flops 2097152 | bytes 4325440 | tf_op jit(solution)/shard_map/convert_element_type | solution.py:69
  211.5 2.7 collective-permute-start.5
  214.2 1.0 collective-permute-start.6
  215.2 10.5 %add_convert_fusion.4 = bf16[512,128]{0,1:T(8,128)(2,1)S(1)} fusion(f32[512,512]{0,1:T(8,128)S(1)} %fusion.9, f32[512,512]{0,1:T(8,128)S(1)} %fusion.13, f32[512,512]{0,1:T(8,128)S(1)} %fusion.17, f32[512,512]{0,1:T(8,128)S(1)} %fusion.21, f32[]{:T(128)} %bitcast.150, f32[]{:T(128)} %bitcast.149, f32[]{:T(128)} %bitcast.148, f32[]{:T(128)} %bitcast.147, ...), kind=kLoop, calls=%fused_computation.79 | loop fusion | flops 2097152 | bytes 4325440 | tf_op jit(solution)/shard_map/convert_element_type | solution.py:69
  225.8 0.4 copy.35
  226.3 2.0 convert_add_fusion
  228.3 1.6 collective-permute-start.7
  229.9 0.9 collective-permute-start.8
  230.8 2.4 collective-permute-start.9
  233.2 1.6 fusion.2
  234.9 2.2 collective-permute-done.7
  237.1 2.9 collective-permute-done.8
  240.0 2.0 collective-permute-done.9
  242.0 1.3 fusion.44
  243.7 0.9 copy-done.5
  244.6 0.5 multiply_reduce_fusion
  245.5 0.3 copy.43
  245.8 6.6 %convolution_convert_fusion = bf16[512,4096]{1,0:T(8,128)(2,1)} fusion(bf16[512,4096]{1,0:T(8,128)(2,1)} %bitcast.277, bf16[64,8,4,128]{3,2,1,0:T(4,128)(2,1)S(1)} %bitcast.296), kind=kOutput, calls=%fused_computation.1 | convolution fusion | flops 2149580800 | bytes 8912896 | tf_op jit(solution)/shard_map/dot_general | solution.py:116
  252.4 35.9 %reduce-scatter.2.cloned.1.call-done = bf16[512,512]{1,0:T(8,128)(2,1)} async-done(((bf16[512,4096]{1,0:T(8,128)(2,1)}), bf16[512,512]{1,0:T(8,128)(2,1)}) %reduce-scatter.2.cloned.1.call-update) | async-done | bytes 524304 | tf_op jit(solution)/shard_map/reduce_scatter | solution.py:117
  (40 shorter events, 1.5 us)
Async XLA Ops:
  9.9 54.2 %all-to-all-start = ((bf16[512,8,512]{2,0,1:T(8,128)(2,1)}), bf16[512,8,512]{2,0,1:T(8,128)(2,1)}, u32[]{:S(2)}, u32[]{:S(2)}) async-start(bf16[512,8,512]{2,0,1:T(8,128)(2,1)} %tile.2), calls=%async_computation | async-start | bytes 8388608 | tf_op jit(solution)/shard_map/all_to_all | solution.py:79
  14.5 273.8 %reduce-scatter.2.cloned.1.call-start = ((), (), s32[]{:S(2)}) async-start(), calls=%async_computation.2 | async-start | bytes 4718592 | tf_op jit(solution)/shard_map/reduce_scatter | solution.py:117
  14.7 1.6 slice-start
  16.3 2.8 slice-start.1
  19.1 1.3 copy-start.6
  19.1 1.3 copy-start.3
  37.4 33.3 %copy-start.2 = (bf16[2,4,1024,128]{2,3,1,0:T(8,128)(2,1)S(1)}, bf16[2,4,1024,128]{2,3,1,0:T(8,128)(2,1)}, u32[]{:S(2)}) copy-start(bf16[2,4,1024,128]{2,3,1,0:T(8,128)(2,1)} %copy.45) | copy-start | bytes 6291460
  70.7 2.7 copy-start
  160.0 16.1 %copy-start.4 = (bf16[1,4,1024,128]{2,3,1,0:T(8,128)(2,1)S(1)}, bf16[1,4,1024,128]{2,3,1,0:T(8,128)(2,1)}, u32[]{:S(2)}) copy-start(bf16[1,4,1024,128]{2,3,1,0:T(8,128)(2,1)} %copy.46) | copy-start | bytes 3145732
  160.4 17.6 %copy-start.1 = (bf16[512,8,512]{0,2,1:T(8,128)(2,1)S(1)}, bf16[512,8,512]{0,2,1:T(8,128)(2,1)}, u32[]{:S(2)}) copy-start(bf16[512,8,512]{0,2,1:T(8,128)(2,1)} %copy.32) | copy-start | bytes 12582916
  161.4 50.1 %collective-permute-start = (bf16[4,128,128]{2,1,0:T(8,128)(2,1)}, bf16[4,128,128]{2,1,0:T(8,128)(2,1)S(1)}, u32[]{:S(2)}, u32[]{:S(2)}) collective-permute-start(bf16[4,128,128]{2,1,0:T(8,128)(2,1)} %get-tuple-element.213), channel_id=1, source_target_pairs={{0,8},{8,16},{16,24},{24,32},{32,40},{40,48},{48,56},{56,0},{64,72... | collective-permute-start | bytes 393224 | tf_op jit(solution)/shard_map/ppermute | solution.py:24
  163.3 50.9 %collective-permute-start.1 = (bf16[4,128,128]{2,1,0:T(8,128)(2,1)}, bf16[4,128,128]{2,1,0:T(8,128)(2,1)S(1)}, u32[]{:S(2)}, u32[]{:S(2)}) collective-permute-start(bf16[4,128,128]{2,1,0:T(8,128)(2,1)} %get-tuple-element.213), channel_id=1, source_target_pairs={{0,16},{8,24},{16,32},{24,40},{32,48},{40,56},{48,0},{56,8},{64,80... | collective-permute-start | bytes 393224 | tf_op jit(solution)/shard_map/ppermute | solution.py:24
  166.6 59.7 %collective-permute-start.2 = (bf16[4,128,128]{2,1,0:T(8,128)(2,1)}, bf16[4,128,128]{2,1,0:T(8,128)(2,1)S(1)}, u32[]{:S(2)}, u32[]{:S(2)}) collective-permute-start(bf16[4,128,128]{2,1,0:T(8,128)(2,1)} %get-tuple-element.213), channel_id=1, source_target_pairs={{0,24},{8,32},{16,40},{24,48},{32,56},{40,0},{48,8},{56,16},{64,88... | collective-permute-start | bytes 393224 | tf_op jit(solution)/shard_map/ppermute | solution.py:24
  170.6 55.6 %collective-permute-start.3 = (bf16[4,128,128]{2,1,0:T(8,128)(2,1)}, bf16[4,128,128]{2,1,0:T(8,128)(2,1)}, u32[]{:S(2)}, u32[]{:S(2)}) collective-permute-start(bf16[4,128,128]{2,1,0:T(8,128)(2,1)} %get-tuple-element.213), channel_id=1, source_target_pairs={{0,32},{8,40},{16,48},{24,56},{32,0},{40,8},{48,16},{56,24},{64,96... | collective-permute-start | bytes 393224 | tf_op jit(solution)/shard_map/ppermute | solution.py:24
  171.1 55.1 %collective-permute-start.4 = (bf16[4,128,128]{2,1,0:T(8,128)(2,1)}, bf16[4,128,128]{2,1,0:T(8,128)(2,1)}, u32[]{:S(2)}, u32[]{:S(2)}) collective-permute-start(bf16[4,128,128]{2,1,0:T(8,128)(2,1)} %get-tuple-element.213), channel_id=1, source_target_pairs={{0,40},{8,48},{16,56},{24,0},{32,8},{40,16},{48,24},{56,32},{64,10... | collective-permute-start | bytes 393224 | tf_op jit(solution)/shard_map/ppermute | solution.py:24
  211.5 14.8 %collective-permute-start.5 = (bf16[4,128,128]{2,1,0:T(8,128)(2,1)}, bf16[4,128,128]{2,1,0:T(8,128)(2,1)}, u32[]{:S(2)}, u32[]{:S(2)}) collective-permute-start(bf16[4,128,128]{2,1,0:T(8,128)(2,1)} %get-tuple-element.213), channel_id=1, source_target_pairs={{0,48},{8,56},{16,0},{24,8},{32,16},{40,24},{48,32},{56,40},{64,11... | collective-permute-start | bytes 393224 | tf_op jit(solution)/shard_map/ppermute | solution.py:24
  214.2 12.1 %collective-permute-start.6 = (bf16[4,128,128]{2,1,0:T(8,128)(2,1)}, bf16[4,128,128]{2,1,0:T(8,128)(2,1)}, u32[]{:S(2)}, u32[]{:S(2)}) collective-permute-start(bf16[4,128,128]{2,1,0:T(8,128)(2,1)} %get-tuple-element.213), channel_id=1, source_target_pairs={{0,56},{8,0},{16,8},{24,16},{32,24},{40,32},{48,40},{56,48},{64,12... | collective-permute-start | bytes 393224 | tf_op jit(solution)/shard_map/ppermute | solution.py:24
  228.3 8.8 %collective-permute-start.7 = (f32[4,128,128]{2,1,0:T(8,128)}, f32[4,128,128]{2,1,0:T(8,128)S(1)}, u32[]{:S(2)}, u32[]{:S(2)}) collective-permute-start(f32[4,128,128]{2,1,0:T(8,128)} %convert_add_fusion), channel_id=1, source_target_pairs={{0,64},{8,72},{16,80},{24,88},{32,96},{40,104},{48,112},{56,120},{... | collective-permute-start | bytes 786440 | tf_op jit(solution)/shard_map/ppermute | solution.py:24
  229.9 10.2 %collective-permute-start.8 = (f32[4,128,128]{2,1,0:T(8,128)}, f32[4,128,128]{2,1,0:T(8,128)S(1)}, u32[]{:S(2)}, u32[]{:S(2)}) collective-permute-start(f32[4,128,128]{2,1,0:T(8,128)} %convert_add_fusion), channel_id=1, source_target_pairs={{0,128},{8,136},{16,144},{24,152},{32,160},{40,168},{48,176},{56,1... | collective-permute-start | bytes 786440 | tf_op jit(solution)/shard_map/ppermute | solution.py:24
  230.8 11.2 %collective-permute-start.9 = (f32[4,128,128]{2,1,0:T(8,128)}, f32[4,128,128]{2,1,0:T(8,128)}, u32[]{:S(2)}, u32[]{:S(2)}) collective-permute-start(f32[4,128,128]{2,1,0:T(8,128)} %convert_add_fusion), channel_id=1, source_target_pairs={{0,192},{8,200},{16,208},{24,216},{32,224},{40,232},{48,240},{56,2... | collective-permute-start | bytes 786440 | tf_op jit(solution)/shard_map/ppermute | solution.py:24
  243.4 1.2 copy-start.5
  244.6 0.7 copy-start.7
Sparse Core Ops, SparseCore 0:
  252.5 35.7 reduce-scatter.1
